TPU v7x, 256 devices: a whole 4x4x8 slice. The times are simulated.
256 devices in a mesh: seq: 64 (over x, z, core), ch: 4 (over y).
Axes of the slice: x: 4, y: 4, z: 8, core: 2. Of those that a mesh axis runs over, the one named last changes fastest.
Arguments:
- inputs: bfloat16 [8192, 4096], P('seq'), may hold values from -6 to 6
- norm_gain: float32 [4096], replicated, may hold values from 0.1 to 1.9
- in_weight: bfloat16 [4096, 3, 1024], P('seq', None, 'ch'), may hold values from -0.09375 to 0.09375
- short_filter: float32 [3, 3, 1024], P(None, None, 'ch'), may hold values from -4 to 4
- long_filter: float32 [8192, 1024], P('seq', 'ch'), may hold values from -2.2 to 2.2
- conv_bias: float32 [1024], P('ch'), may hold values from -4 to 4
- out_weight: bfloat16 [1024, 4096], P('ch', 'seq'), may hold values from -0.1875 to 0.1875
- out_grad: bfloat16 [8192, 4096], P('seq'), may hold values from -6 to 6
Outputs:
- block_out: bfloat16 [8192, 4096], P('seq', 'ch')
- in_grad: bfloat16 [8192, 4096], P('seq')
- filter_grad: float32 [8192, 1024], P('seq', 'ch')
All inputs are finite; a program needn't handle non-finite values.
Results may differ from a plain program's by a relative error of at most 0.013.
Values may be sent and summed in bfloat16 or wider, within the bound.
No kernel may reach another device: no remote copies, remote signals or barrier semaphores. Data moves between devices by JAX's collectives and lax.ppermute only.
A program may use at most 64 MiB of HBM per device.

v0:
```python
import math
import jax
import jax.numpy as jnp
from jax import lax
from jax.sharding import PartitionSpec as P

epsilon = 1e-05
highest = lax.Precision.HIGHEST


def passed_along(block, axis, distance):
    devices = range(lax.axis_size(axis))
    route = [(i - distance, i) for i in devices if i - distance in devices]
    return lax.ppermute(block, axis, route)


def to_columns(signals):
    return lax.all_to_all(signals, "seq", split_axis=1, concat_axis=2, tiled=True)


def to_rows(signals):
    return lax.all_to_all(signals, "seq", split_axis=2, concat_axis=1, tiled=True)


def turn_table(rows, cols, period, sign):
    turns = jnp.arange(rows, dtype=jnp.int32)[:, None] * jnp.arange(cols, dtype=jnp.int32)[None, :]
    phases = sign * 2.0 * math.pi / period * (turns % period).astype(jnp.float32)
    return (jnp.cos(phases), jnp.sin(phases))


def fft_sizes(seq_total):
    total = 2 * seq_total
    inner = 1
    while inner * inner < total:
        inner *= 2
    return (total // inner, inner)


def forward_dft(signals):
    count, chans, seq_total = signals.shape
    outer, inner = fft_sizes(seq_total)
    grid = signals.reshape(count, chans, outer // 2, inner)
    cos_out, sin_out = turn_table(outer, outer // 2, outer, 1.0)
    first_real = jnp.einsum("kn,ucnm->uckm", cos_out, grid, precision=highest)
    first_imag = -jnp.einsum("kn,ucnm->uckm", sin_out, grid, precision=highest)
    cos_tw, sin_tw = turn_table(outer, inner, outer * inner, 1.0)
    turned_real = first_real * cos_tw + first_imag * sin_tw
    turned_imag = first_imag * cos_tw - first_real * sin_tw
    cos_in, sin_in = turn_table(inner, inner, inner, 1.0)
    spec_real = jnp.einsum("uckm,mj->uckj", turned_real, cos_in, precision=highest) + jnp.einsum(
        "uckm,mj->uckj", turned_imag, sin_in, precision=highest
    )
    spec_imag = jnp.einsum("uckm,mj->uckj", turned_imag, cos_in, precision=highest) - jnp.einsum(
        "uckm,mj->uckj", turned_real, sin_in, precision=highest
    )
    return (spec_real, spec_imag)


def inverse_dft(spec_real, spec_imag):
    count, chans, outer, inner = spec_real.shape
    cos_in, sin_in = turn_table(inner, inner, inner, 1.0)
    back_real = jnp.einsum("uckj,jm->uckm", spec_real, cos_in, precision=highest) - jnp.einsum(
        "uckj,jm->uckm", spec_imag, sin_in, precision=highest
    )
    back_imag = jnp.einsum("uckj,jm->uckm", spec_imag, cos_in, precision=highest) + jnp.einsum(
        "uckj,jm->uckm", spec_real, sin_in, precision=highest
    )
    cos_tw, sin_tw = turn_table(outer, inner, outer * inner, 1.0)
    turned_real = back_real * cos_tw - back_imag * sin_tw
    turned_imag = back_imag * cos_tw + back_real * sin_tw
    cos_out, sin_out = turn_table(outer, outer // 2, outer, 1.0)
    grid = jnp.einsum("kn,uckm->ucnm", cos_out, turned_real, precision=highest) - jnp.einsum(
        "kn,uckm->ucnm", sin_out, turned_imag, precision=highest
    )
    return grid.reshape(count, chans, outer * inner // 2) / float(outer * inner)


def per_device(
    inputs, norm_gain, in_weight, short_filter, long_filter, conv_bias, out_weight, out_grad
):
    local_rows = inputs.shape[0]
    model_width = inputs.shape[1]
    slab_width = long_filter.shape[1]
    taps = short_filter.shape[1]
    wide_inputs = inputs.astype(jnp.float32)
    inv_rms = lax.rsqrt(jnp.mean(wide_inputs * wide_inputs, axis=1, keepdims=True) + epsilon)
    normed = (wide_inputs * inv_rms * norm_gain).astype(jnp.bfloat16)
    in_panel, out_panel = (
        lax.all_gather(in_weight, "seq", axis=0, tiled=True),
        lax.all_gather(out_weight, "seq", axis=1, tiled=True),
    )
    in_flat = in_panel.reshape(model_width, 3 * slab_width)
    projected = jnp.dot(normed, in_flat, preferred_element_type=jnp.float32)
    projected = projected.astype(jnp.bfloat16).reshape(local_rows, 3, slab_width)
    upper_rim = passed_along(projected[local_rows - (taps - 1) :], "seq", 1)
    extended = jnp.concatenate([upper_rim, projected], 0).astype(jnp.float32)
    mixed = jnp.zeros((local_rows, 3, slab_width), jnp.float32)
    for offset in range(taps):
        begin = taps - 1 - offset
        mixed = mixed + short_filter[:, offset, :][None] * extended[begin : begin + local_rows]
    query_br = mixed[:, 0]
    key_br = mixed[:, 1]
    value_br = mixed[:, 2]
    product = key_br * value_br
    gate_grad = jnp.dot(out_grad, out_panel.T, preferred_element_type=jnp.float32)
    carried = gate_grad * query_br
    columns = to_columns(jnp.stack([product, long_filter, carried]).transpose(0, 2, 1))
    all_real, all_imag = forward_dft(columns)
    sig_real, filt_real, grad_real = (all_real[0], all_real[1], all_real[2])
    sig_imag, filt_imag, grad_imag = (all_imag[0], all_imag[1], all_imag[2])
    conv_real = sig_real * filt_real - sig_imag * filt_imag
    conv_imag = sig_real * filt_imag + sig_imag * filt_real
    back_real = grad_real * filt_real + grad_imag * filt_imag
    back_imag = grad_imag * filt_real - grad_real * filt_imag
    pair_real = grad_real * sig_real + grad_imag * sig_imag
    pair_imag = grad_imag * sig_real - grad_real * sig_imag
    outs = inverse_dft(
        jnp.stack([conv_real, back_real, pair_real]), jnp.stack([conv_imag, back_imag, pair_imag])
    )
    returned = to_rows(outs).transpose(0, 2, 1)
    conv_out = returned[0]
    back_conv = returned[1]
    filter_grad = returned[2] * float(local_rows * lax.axis_size("seq")) ** (-0.5)
    biased = conv_out + conv_bias * product
    gated = (query_br * biased).astype(jnp.bfloat16)
    partial_out = jnp.dot(gated, out_panel, preferred_element_type=jnp.float32)
    summed = lax.psum_scatter(
        partial_out.astype(jnp.bfloat16), "ch", scatter_dimension=1, tiled=True
    ).astype(jnp.float32)
    share = summed.shape[1]
    residual = lax.dynamic_slice_in_dim(wide_inputs, lax.axis_index("ch") * share, share, 1)
    block_out = (residual + summed).astype(jnp.bfloat16)
    source_grad = back_conv + conv_bias * carried
    mixed_grad = jnp.stack([gate_grad * biased, source_grad * value_br, source_grad * key_br], 1)
    lower_rim = passed_along(mixed_grad[: taps - 1], "seq", -1)
    extended_back = jnp.concatenate([mixed_grad, lower_rim], 0)
    proj_grad = jnp.zeros((local_rows, 3, slab_width), jnp.float32)
    for offset in range(taps):
        proj_grad = (
            proj_grad
            + short_filter[:, offset, :][None] * extended_back[offset : offset + local_rows]
        )
    proj_grad = proj_grad.astype(jnp.bfloat16).reshape(local_rows, 3 * slab_width)
    partial_grad = jnp.dot(proj_grad, in_flat.T, preferred_element_type=jnp.float32)
    norm_grad = lax.psum(partial_grad, "ch")
    weighted = norm_grad * norm_gain
    inner_term = jnp.mean(weighted * wide_inputs, axis=1, keepdims=True)
    in_grad = (
        out_grad.astype(jnp.float32) + weighted * inv_rms - wide_inputs * inv_rms**3 * inner_term
    ).astype(jnp.bfloat16)
    return (block_out, in_grad, filter_grad)


def solution(mesh):
    return jax.shard_map(
        per_device,
        mesh=mesh,
        in_specs=(
            P("seq", None),
            P(),
            P("seq", None, "ch"),
            P(None, None, "ch"),
            P("seq", "ch"),
            P("ch"),
            P("ch", "seq"),
            P("seq", None),
        ),
        out_specs=(P("seq", "ch"), P("seq", None), P("seq", "ch")),
        check_vma=False,
    )
```

profile of v0, /device:TPU:1, one launch (start us, length us, event | category | flops | bytes accessed | tf_op | source)
XLA Modules:
  0.0 393.4 jit_solution(6677568835043596494)
XLA Ops:
  7.2 0.0 all-gather.3.cloned.1.call-start
  7.2 0.7 all-gather.3.cloned.1.call-update
  7.9 0.0 all-gather.5.cloned.1.call-start
  7.9 0.7 all-gather.5.cloned.1.call-update
  8.6 0.8 fusion.142
  9.5 1.5 multiply_reduce_fusion.1
  11.0 0.6 multiply_multiply_fusion
  11.6 83.9 %all-gather.3.cloned.1.call-done = bf16[4096,3,256]{2,0,1:T(8,128)(2,1)} async-done(((bf16[64,3,256]{2,0,1:T(8,128)(2,1)}), bf16[4096,3,256]{2,0,1:T(8,128)(2,1)}) %all-gather.3.cloned.1.call-update) | async-done | bytes 6291472 | tf_op jit(solution)/shard_map/all_gather | solution.py:89
  95.5 8.7 %copy.46 = bf16[4096,3,256]{0,2,1:T(8,128)(2,1)} copy(bf16[4096,3,256]{2,0,1:T(8,128)(2,1)} %all-gather.3.cloned.1.call-done) | data formatting | bytes 12582912 | tf_op jit(solution)/shard_map/all_gather | solution.py:89
  104.2 5.1 %convolution_convert_fusion.1 = bf16[128,768]{1,0:T(8,128)(2,1)S(1)} fusion(bf16[4096,768]{0,1:T(8,128)(2,1)} %bitcast.127, bf16[128,4096]{1,0:T(8,128)(2,1)S(1)} %copy-done, f32[4096]{0:T(1024)S(1)} %copy-done.9, f32[128]{0:T(128)S(1)} %get-tuple-element.19), kind=kOutput, calls=%fused_computation.16 | convolution fusion | flops 807501824 | bytes 7553536 | tf_op jit(solution)/shard_map/dot_general | solution.py:93
  109.3 2.7 collective-permute-start
  112.1 60.2 %all-gather.5.cloned.1.call-done = bf16[256,4096]{0,1:T(8,128)(2,1)} async-done(((bf16[256,64]{0,1:T(8,128)(2,1)}), bf16[256,4096]{0,1:T(8,128)(2,1)}) %all-gather.5.cloned.1.call-update) | async-done | bytes 2097168 | tf_op jit(solution)/shard_map/all_gather | solution.py:90
  172.3 2.0 fusion.143
  174.4 0.2 copy.48
  174.6 0.2 copy.49
  174.8 0.1 fusion.17
  175.0 0.4 copy-done.8
  175.4 1.0 copy.50
  176.4 6.6 %all-to-all-start = ((f32[3,256,128]{2,0,1:T(4,128)}), f32[3,256,128]{2,0,1:T(4,128)S(1)}, u32[]{:S(2)}, u32[]{:S(2)}) async-start(f32[3,256,128]{2,0,1:T(4,128)} %copy.50), calls=%async_computation | async-start | bytes 1048576 | tf_op jit(solution)/shard_map/all_to_all | solution.py:18
  183.0 0.2 reduce-scatter.2.cloned.1.call-start
  183.2 0.3 fusion.78
  183.5 0.1 copy.53
  183.6 0.3 fusion.77
  183.8 0.1 copy.54
  183.9 16.3 %all-to-all-done = f32[3,256,128]{2,0,1:T(4,128)S(1)} async-done(((f32[3,256,128]{2,0,1:T(4,128)}), f32[3,256,128]{2,0,1:T(4,128)S(1)}, u32[]{:S(2)}, u32[]{:S(2)}) %all-to-all-start) | async-done | bytes 393248 | tf_op jit(solution)/shard_map/all_to_all | solution.py:18
  200.3 1.5 convolution_bitcast_fusion.1
  201.8 1.5 fusion
  203.3 1.6 fusion.31
  204.9 1.6 fusion.32
  206.5 1.6 convolution_add_fusion.1
  208.1 1.6 convolution_subtract_fusion.1
  209.7 0.1 multiply_add_fusion.3
  209.8 0.1 multiply_subtract_fusion.3
  209.9 1.1 fusion.13
  211.0 1.3 fusion.12
  212.4 1.1 convolution_subtract_fusion
  213.5 1.1 convolution_add_fusion
  214.6 1.2 fusion.8
  215.8 1.2 fusion.2
  217.0 8.6 %copy.85 = f32[3,4,64,128]{1,0,3,2:T(4,128)} copy(f32[3,4,64,128]{3,2,1,0:T(8,128)S(1)} %fusion.2) | data formatting | bytes 786432 | tf_op jit(solution)/shard_map/div | solution.py:75
  225.6 16.0 %reshape.105 = f32[64,1,1536]{2,1,0:T(1,128)S(1)} reshape(f32[8192,3,4]{2,1,0:T(4,128)} %bitcast.125) | data formatting | bytes 786432
  241.6 20.6 %all_to_all.33 = f32[64,1,1536]{2,1,0:T(1,128)S(1)} all-to-all(f32[64,1,1536]{2,1,0:T(1,128)S(1)} %reshape.105), channel_id=1, replica_groups=mesh['seq'=64,'ch'=4] {'seq'}, dimensions={0} | all-to-all | bytes 786432 | tf_op jit(solution)/shard_map/all_to_all | solution.py:22
  262.3 0.5 broadcast.224
  262.8 1.6 reduce
  264.4 11.6 %reshape.106 = f32[8192,3,4]{2,1,0:T(4,128)} reshape(f32[64,1536]{1,0:T(8,128)S(1)} %reduce) | data formatting | bytes 786432
  275.9 10.1 %copy.86 = f32[3,4,64,128]{3,2,1,0:T(8,128)} copy(f32[3,4,64,128]{1,0,3,2:T(4,128)} %bitcast.126) | data formatting | bytes 786432 | tf_op jit(solution)/shard_map/all_to_all | solution.py:22
  286.0 2.2 copy.67
  288.1 1.9 copy.68
  290.0 1.8 fusion.37
  291.9 1.8 convolution_convert_fusion
  293.7 0.0 all-reduce.2.cloned.1.call-start
  293.7 1.0 fusion.38
  294.7 1.0 pad_maximum_fusion.7
  295.7 2.6 collective-permute-start.1
  298.3 2.4 collective-permute-done.1
  300.7 6.4 %convolution_bitcast_fusion = f32[128,4096]{1,0:T(8,128)} fusion(bf16[4096,3,256]{2,0,1:T(8,128)(2,1)} %all-gather.3.cloned.1.call-done, f32[130,3,256]{2,0,1:T(8,128)S(1)} %pad_maximum_fusion.6, f32[3,256]{1,0:T(4,128)S(1)} %get-tuple-element.20, f32[3,256]{1,0:T(4,128)S(1)} %get-tuple-element.21, f32[3,256]{1,0:T(4,128)S(1)} %bitcast.136, ...), kind=kOutput, calls=%fused_computation | convolution fusion | flops 806092800 | bytes 9580544 | tf_op jit(solution)/shard_map/dot_general | solution.py:144
  307.2 1.6 convert_element_type.86
  308.7 1.6 fusion.33
  310.3 5.3 %reduce-scatter.2.cloned.1.call-done = bf16[128,1024]{1,0:T(8,128)(2,1)} async-done(((bf16[128,4096]{1,0:T(8,128)(2,1)}), bf16[128,1024]{1,0:T(8,128)(2,1)}) %reduce-scatter.2.cloned.1.call-update) | async-done | bytes 262160 | tf_op jit(solution)/shard_map/reduce_scatter | solution.py:127
  315.6 1.9 add_convert_fusion
  317.5 65.3 %all-reduce.2.cloned.1.call-done = f32[128,4096]{1,0:T(8,128)} async-done(((f32[128,4096]{1,0:T(8,128)}), f32[128,4096]{1,0:T(8,128)}) %all-reduce.2.cloned.1.call-update) | async-done | bytes 2097168 | tf_op jit(solution)/shard_map/psum | solution.py:145
  382.8 2.1 multiply_reduce_fusion
  384.9 0.1 copy-done.2
  385.0 1.9 subtract_convert_fusion
  (41 shorter events, 0.3 us)
Async XLA Ops:
  7.2 88.3 %all-gather.3.cloned.1.call-start = ((), (), s32[]{:S(2)}) async-start(), calls=%async_computation.3 | async-start | bytes 6389760 | tf_op jit(solution)/shard_map/all_gather | solution.py:89
  7.9 164.4 %all-gather.5.cloned.1.call-start = ((), (), s32[]{:S(2)}) async-start(), calls=%async_computation.4 | async-start | bytes 2129920 | tf_op jit(solution)/shard_map/all_gather | solution.py:90
  11.6 92.6 %copy-start.13 = (f32[128]{0:T(128)}, f32[128]{0:T(128)S(1)}, u32[]{:S(2)}) copy-start(f32[128]{0:T(128)S(1)} %get-tuple-element.19) | copy-start | bytes 1540
  11.6 92.6 %copy-start = (bf16[128,4096]{1,0:T(8,128)(2,1)S(1)}, bf16[128,4096]{1,0:T(8,128)(2,1)}, u32[]{:S(2)}) copy-start(bf16[128,4096]{1,0:T(8,128)(2,1)} %param.8) | copy-start | bytes 3145732
  11.6 92.6 %copy-start.9 = (f32[4096]{0:T(1024)S(1)}, f32[4096]{0:T(1024)}, u32[]{:S(2)}) copy-start(f32[4096]{0:T(1024)} %param.9) | copy-start | bytes 49156
  104.2 68.1 %copy-start.3 = (bf16[128,4096]{1,0:T(8,128)(2,1)S(1)}, bf16[128,4096]{1,0:T(8,128)(2,1)}, u32[]{:S(2)}) copy-start(bf16[128,4096]{1,0:T(8,128)(2,1)} %param.15) | copy-start | bytes 3145732
  109.3 65.4 %collective-permute-start = (bf16[2,3,256]{2,0,1:T(2,128)(2,1)S(1)}, bf16[2,3,256]{2,0,1:T(2,128)(2,1)S(1)}, u32[]{:S(2)}, u32[]{:S(2)}) collective-permute-start(bf16[2,3,256]{2,0,1:T(2,128)(2,1)S(1)} %bitcast.138), channel_id=1, source_target_pairs={{0,4},{4,8},{8,12},{12,16},{16,20},{20,24},{24,28},{28,32},{32,36}... | collective-permute-start | bytes 9224 | tf_op jit(solution)/shard_map/ppermute | solution.py:14
  174.4 1.0 copy-start.7
  174.4 1.0 copy-start.8
  176.4 23.9 %all-to-all-start = ((f32[3,256,128]{2,0,1:T(4,128)}), f32[3,256,128]{2,0,1:T(4,128)S(1)}, u32[]{:S(2)}, u32[]{:S(2)}) async-start(f32[3,256,128]{2,0,1:T(4,128)} %copy.50), calls=%async_computation | async-start | bytes 1048576 | tf_op jit(solution)/shard_map/all_to_all | solution.py:18
  183.0 132.6 %reduce-scatter.2.cloned.1.call-start = ((), (), s32[]{:S(2)}) async-start(), calls=%async_computation.5 | async-start | bytes 1310720 | tf_op jit(solution)/shard_map/reduce_scatter | solution.py:127
  275.9 14.1 %copy-start.11 = (f32[256]{0:T(256)S(1)}, f32[256]{0:T(256)}, u32[]{:S(2)}) copy-start(f32[256]{0:T(256)} %param.13) | copy-start | bytes 3076
  286.0 5.9 %copy-start.1 = (bf16[256,4096]{0,1:T(8,128)(2,1)S(1)}, bf16[256,4096]{0,1:T(8,128)(2,1)}, u32[]{:S(2)}) copy-start(bf16[256,4096]{0,1:T(8,128)(2,1)} %all-gather.5.cloned.1.call-done) | copy-start | bytes 6291460
  293.6 7.0 %copy-start.5 = (f32[128,1,256]{2,0,1:T(8,128)S(1)}, f32[128,1,256]{2,0,1:T(8,128)}, u32[]{:S(2)}) copy-start(f32[128,1,256]{2,0,1:T(8,128)} %get-tuple-element.5) | copy-start | bytes 393220
  293.6 7.0 %copy-start.6 = (f32[128,1,256]{2,0,1:T(8,128)S(1)}, f32[128,1,256]{2,0,1:T(8,128)}, u32[]{:S(2)}) copy-start(f32[128,1,256]{2,0,1:T(8,128)} %get-tuple-element.13) | copy-start | bytes 393220
  293.7 89.1 %all-reduce.2.cloned.1.call-start = ((), (), s32[]{:S(2)}) async-start(), calls=%async_computation.6 | async-start | bytes 4194304 | tf_op jit(solution)/shard_map/psum | solution.py:145
  295.7 4.9 %collective-permute-start.1 = (f32[2,3,256]{2,0,1:T(2,128)S(1)}, f32[2,3,256]{2,0,1:T(2,128)S(1)}, u32[]{:S(2)}, u32[]{:S(2)}) collective-permute-start(f32[2,3,256]{2,0,1:T(2,128)S(1)} %slice.110), channel_id=1, source_target_pairs={{4,0},{8,4},{12,8},{16,12},{20,16},{24,20},{28,24},{32,28},{36,32}... | collective-permute-start | bytes 18440 | tf_op jit(solution)/shard_map/ppermute | solution.py:14
  307.1 75.6 %copy-start.10 = (f32[4096]{0:T(1024)S(1)}, f32[4096]{0:T(1024)}, u32[]{:S(2)}) copy-start(f32[4096]{0:T(1024)} %param.9) | copy-start | bytes 49156
  310.3 74.6 %copy-start.4 = (bf16[128,4096]{1,0:T(8,128)(2,1)S(1)}, bf16[128,4096]{1,0:T(8,128)(2,1)}, u32[]{:S(2)}) copy-start(bf16[128,4096]{1,0:T(8,128)(2,1)} %param.15) | copy-start | bytes 3145732
  310.3 74.6 %copy-start.12 = (f32[128]{0:T(128)S(1)}, f32[128]{0:T(128)}, u32[]{:S(2)}) copy-start(f32[128]{0:T(128)} %get-tuple-element.18) | copy-start | bytes 1540
  310.3 74.6 %copy-start.14 = (f32[128]{0:T(128)S(1)}, f32[128]{0:T(128)}, u32[]{:S(2)}) copy-start(f32[128]{0:T(128)} %copy-done.13) | copy-start | bytes 1540
  382.8 2.2 copy-start.2
Sparse Core Ops, SparseCore 0:
  10.8 84.6 all-gather.2
  98.3 74.0 all-gather.4
  293.8 21.7 reduce-scatter.1
  317.8 64.9 all-reduce.1
where the time goes:
time: 395 us; the launch traced here: 393 us
  waiting for transfers between devices  235 us (59%)
  local copies, waits for them, and re-layouts  62.4 us (16%)
  matrix products  31.7 us (8%)
  blocking collectives  20.6 us (5%)
  other arithmetic  17.5 us (4%)
  between operations  14.1 us (4%)
  starting transfers between devices  12.2 us (3%)
    all_gather x1, waiting for transfers between devices, per_device(): lax.all_gather(in_weight, 'seq', axis=0, tiled=True)  83.9 us
    psum x1, waiting for transfers between devices, per_device(): norm_grad = lax.psum(partial_grad, 'ch')  65.3 us
    all_gather x1, waiting for transfers between devices, per_device(): lax.all_gather(out_weight, 'seq', axis=1, tiled=True)  60.2 us
    unnamed x34, local copies, waits for them, and re-layouts  28.1 us
    all_to_all x1, blocking collectives, to_rows(): lax.all_to_all(signals, 'seq', split_axis=2, concat_axis=1, tiled=True)  20.6 us
    all_to_all x1, waiting for transfers between devices, to_columns(): lax.all_to_all(signals, 'seq', split_axis=1, concat_axis=2, tiled=True)  16.3 us
    all_to_all x4, local copies, waits for them, and re-layouts, to_rows(): lax.all_to_all(signals, 'seq', split_axis=2, concat_axis=1, tiled=True)  14.6 us
    all_gather x1, local copies, waits for them, and re-layouts, per_device(): lax.all_gather(in_weight, 'seq', axis=0, tiled=True)  8.7 us
  transfers between devices with their start and end apart: 7, of which 6 were waited for; matrix products, arithmetic and copies ran while one was open for 8% of the time, Pallas kernels for 0%

commit v1 on v0

--- a/solution.py
+++ b/solution.py
@@ -6,6 +6,15 @@
 
 epsilon = 1e-05
 highest = lax.Precision.HIGHEST
+start_the_grid = lambda matrix: jnp.concatenate(
+    lax.all_to_all(
+        jnp.stack(jnp.split(matrix, lax.axis_size("seq"), 2)),
+        axis_name="seq",
+        split_axis=0,
+        concat_axis=0,
+    ),
+    axis=1,
+)
 
 
 def passed_along(block, axis, distance):
@@ -19,7 +28,7 @@
 
 
 def to_rows(signals):
-    return lax.all_to_all(signals, "seq", split_axis=2, concat_axis=1, tiled=True)
+    return start_the_grid(signals)
 
 
 def turn_table(rows, cols, period, sign):

time: 395 us -> 376 us (0.952)
  local copies, waits for them, and re-layouts: 62.4 us -> 44.6 us
    all_to_all x4 -> x0, local copies, waits for them, and re-layouts: 14.6 us -> none  [to_rows(): lax.all_to_all(signals, 'seq', split_axis=2, concat_axis=1, tiled=True)]
    div x1, local copies, waits for them, and re-layouts: 8.64 us -> 0.15 us  [inverse_dft(): return grid.reshape(count, chans, outer * inner // 2) / float(outer * inner)]
    unnamed x34 -> x97, local copies, waits for them, and re-layouts: 28.1 us -> 30 us
  transfers between devices with their start and end apart: 7 -> 7, of which waited for: 6 -> 6; matrix products, arithmetic and copies ran while one was open for 8% -> 9% of each run, Pallas kernels for 0% -> 0%
where the time goes in v1:
time: 376 us; the launch traced here: 374 us
  waiting for transfers between devices  235 us (62%)
  local copies, waits for them, and re-layouts  44.6 us (12%)
  matrix products  31.8 us (8%)
  blocking collectives  20.6 us (5%)
  other arithmetic  15.8 us (4%)
  between operations  14.2 us (4%)
  starting transfers between devices  12 us (3%)
    all_gather x1, waiting for transfers between devices, per_device(): lax.all_gather(in_weight, 'seq', axis=0, tiled=True)  83.9 us
    psum x1, waiting for transfers between devices, per_device(): norm_grad = lax.psum(partial_grad, 'ch')  65.4 us
    all_gather x1, waiting for transfers between devices, per_device(): lax.all_gather(out_weight, 'seq', axis=1, tiled=True)  60.2 us
    unnamed x97, local copies, waits for them, and re-layouts  30 us
    all_to_all x1, blocking collectives, lax.all_to_all(jnp.stack(jnp.split(matrix, lax.axis_size('seq'), 2)), axi...  20.6 us
    all_to_all x1, waiting for transfers between devices, to_columns(): lax.all_to_all(signals, 'seq', split_axis=1, concat_axis=2, tiled=True)  16.3 us
    all_gather x1, local copies, waits for them, and re-layouts, per_device(): lax.all_gather(in_weight, 'seq', axis=0, tiled=True)  8.72 us
  transfers between devices with their start and end apart: 7, of which 6 were waited for; matrix products, arithmetic and copies ran while one was open for 9% of the time, Pallas kernels for 0%

profile of v1, /device:TPU:1, one launch (start us, length us, event | category | flops | bytes accessed | tf_op | source)
XLA Modules:
  0.0 374.2 jit_solution(1003825920578293716)
XLA Ops:
  8.6 0.8 fusion.142
  9.5 1.5 multiply_reduce_fusion.1
  11.6 83.9 %all-gather.3.cloned.1.call-done = bf16[4096,3,256]{2,0,1:T(8,128)(2,1)} async-done(((bf16[64,3,256]{2,0,1:T(8,128)(2,1)}), bf16[4096,3,256]{2,0,1:T(8,128)(2,1)}) %all-gather.3.cloned.1.call-update) | async-done | bytes 6291472 | tf_op jit(solution)/shard_map/all_gather | solution.py:98
  95.5 8.7 %copy.172 = bf16[4096,3,256]{0,2,1:T(8,128)(2,1)} copy(bf16[4096,3,256]{2,0,1:T(8,128)(2,1)} %all-gather.3.cloned.1.call-done) | data formatting | bytes 12582912 | tf_op jit(solution)/shard_map/all_gather | solution.py:98
  104.2 5.1 %convolution_convert_fusion.1 = bf16[128,768]{1,0:T(8,128)(2,1)S(1)} fusion(bf16[4096,768]{0,1:T(8,128)(2,1)} %bitcast.379, bf16[128,4096]{1,0:T(8,128)(2,1)S(1)} %copy-done, f32[4096]{0:T(1024)S(1)} %copy-done.10, f32[128]{0:T(128)S(1)} %get-tuple-element.19), kind=kOutput, calls=%fused_computation.16 | convolution fusion | flops 807501824 | bytes 7553536 | tf_op jit(solution)/shard_map/dot_general | solution.py:102
  109.4 2.7 collective-permute-start
  112.1 60.2 %all-gather.5.cloned.1.call-done = bf16[256,4096]{0,1:T(8,128)(2,1)} async-done(((bf16[256,64]{0,1:T(8,128)(2,1)}), bf16[256,4096]{0,1:T(8,128)(2,1)}) %all-gather.5.cloned.1.call-update) | async-done | bytes 2097168 | tf_op jit(solution)/shard_map/all_gather | solution.py:99
  172.3 2.0 fusion.143
  175.4 1.0 copy.176
  176.4 6.6 %all-to-all-start = ((f32[3,256,128]{2,0,1:T(4,128)}), f32[3,256,128]{2,0,1:T(4,128)S(1)}, u32[]{:S(2)}, u32[]{:S(2)}) async-start(f32[3,256,128]{2,0,1:T(4,128)} %copy.176), calls=%async_computation | async-start | bytes 1048576 | tf_op jit(solution)/shard_map/all_to_all | solution.py:27
  183.9 16.3 %all-to-all-done = f32[3,256,128]{2,0,1:T(4,128)S(1)} async-done(((f32[3,256,128]{2,0,1:T(4,128)}), f32[3,256,128]{2,0,1:T(4,128)S(1)}, u32[]{:S(2)}, u32[]{:S(2)}) %all-to-all-start) | async-done | bytes 393248 | tf_op jit(solution)/shard_map/all_to_all | solution.py:27
  200.3 1.5 convolution_bitcast_fusion.1
  201.8 1.5 fusion
  203.3 1.6 fusion.31
  204.9 1.6 fusion.32
  206.5 1.6 convolution_add_fusion.1
  208.1 1.6 convolution_subtract_fusion.1
  209.9 1.1 fusion.13
  211.0 1.3 fusion.12
  212.4 1.1 convolution_subtract_fusion
  213.5 1.1 convolution_add_fusion
  214.6 1.2 fusion.8
  215.8 1.2 fusion.2
  217.9 0.8 constant_dynamic-update-slice_fusion.41
  218.7 0.7 constant_dynamic-update-slice_fusion.40
  222.9 0.7 constant_dynamic-update-slice_fusion.34
  223.6 0.7 constant_dynamic-update-slice_fusion.33
  224.3 0.7 constant_dynamic-update-slice_fusion.32
  225.0 0.7 constant_dynamic-update-slice_fusion.31
  225.7 0.7 constant_dynamic-update-slice_fusion.30
  226.4 0.7 constant_dynamic-update-slice_fusion.29
  227.1 0.7 constant_dynamic-update-slice_fusion.28
  227.8 0.7 constant_dynamic-update-slice_fusion.27
  228.5 0.7 constant_dynamic-update-slice_fusion.26
  229.2 0.7 constant_dynamic-update-slice_fusion.25
  229.9 0.7 constant_dynamic-update-slice_fusion.24
  230.6 0.7 constant_dynamic-update-slice_fusion.23
  231.3 0.7 constant_dynamic-update-slice_fusion.22
  232.0 0.7 constant_dynamic-update-slice_fusion.21
  236.2 0.7 constant_dynamic-update-slice_fusion.15
  236.9 0.7 constant_dynamic-update-slice_fusion.14
  237.6 0.7 constant_dynamic-update-slice_fusion.13
  238.3 0.7 constant_dynamic-update-slice_fusion.12
  239.0 0.7 constant_dynamic-update-slice_fusion.11
  239.7 0.7 constant_dynamic-update-slice_fusion.10
  242.5 0.7 constant_dynamic-update-slice_fusion.6
  246.7 0.7 constant_dynamic-update-slice_fusion
  247.4 20.6 %all_to_all.20 = f32[64,3,4,128]{3,2,1,0:T(4,128)S(1)} all-to-all(f32[64,3,4,128]{3,2,1,0:T(4,128)S(1)} %constant_dynamic-update-slice_fusion), channel_id=1, replica_groups=mesh['seq'=64,'ch'=4] {'seq'}, dimensions={0} | all-to-all | bytes 786432 | tf_op jit(solution)/shard_map/all_to_all | solution.py:10
  268.0 0.8 copy.191
  268.8 1.9 copy.192
  270.8 1.8 fusion.37
  272.6 1.8 convolution_convert_fusion
  274.5 1.0 fusion.38
  275.4 1.0 pad_maximum_fusion.7
  276.5 2.3 collective-permute-start.1
  278.8 2.6 collective-permute-done.1
  281.4 6.5 %convolution_bitcast_fusion = f32[128,4096]{1,0:T(8,128)} fusion(bf16[4096,3,256]{2,0,1:T(8,128)(2,1)} %all-gather.3.cloned.1.call-done, f32[130,3,256]{2,0,1:T(8,128)S(1)} %pad_maximum_fusion.6, f32[3,256]{1,0:T(4,128)S(1)} %get-tuple-element.20, f32[3,256]{1,0:T(4,128)S(1)} %get-tuple-element.21, f32[3,256]{1,0:T(4,128)S(1)} %bitcast.388, ...), kind=kOutput, calls=%fused_computation | convolution fusion | flops 806092800 | bytes 9580544 | tf_op jit(solution)/shard_map/dot_general | solution.py:153
  288.0 1.5 convert_element_type.86
  289.5 1.6 fusion.33
  291.1 5.2 %reduce-scatter.2.cloned.1.call-done = bf16[128,1024]{1,0:T(8,128)(2,1)} async-done(((bf16[128,4096]{1,0:T(8,128)(2,1)}), bf16[128,1024]{1,0:T(8,128)(2,1)}) %reduce-scatter.2.cloned.1.call-update) | async-done | bytes 262160 | tf_op jit(solution)/shard_map/reduce_scatter | solution.py:136
  296.3 1.9 add_convert_fusion
  298.1 65.4 %all-reduce.2.cloned.1.call-done = f32[128,4096]{1,0:T(8,128)} async-done(((f32[128,4096]{1,0:T(8,128)}), f32[128,4096]{1,0:T(8,128)}) %all-reduce.2.cloned.1.call-update) | async-done | bytes 2097168 | tf_op jit(solution)/shard_map/psum | solution.py:154
  363.5 2.1 multiply_reduce_fusion
  365.7 1.9 subtract_convert_fusion
  (102 shorter events, 17.7 us)
Async XLA Ops:
  7.2 88.3 %all-gather.3.cloned.1.call-start = ((), (), s32[]{:S(2)}) async-start(), calls=%async_computation.3 | async-start | bytes 6389760 | tf_op jit(solution)/shard_map/all_gather | solution.py:98
  7.9 164.4 %all-gather.5.cloned.1.call-start = ((), (), s32[]{:S(2)}) async-start(), calls=%async_computation.4 | async-start | bytes 2129920 | tf_op jit(solution)/shard_map/all_gather | solution.py:99
  11.6 92.7 %copy-start.14 = (f32[128]{0:T(128)}, f32[128]{0:T(128)S(1)}, u32[]{:S(2)}) copy-start(f32[128]{0:T(128)S(1)} %get-tuple-element.19) | copy-start | bytes 1540
  11.6 92.7 %copy-start = (bf16[128,4096]{1,0:T(8,128)(2,1)S(1)}, bf16[128,4096]{1,0:T(8,128)(2,1)}, u32[]{:S(2)}) copy-start(bf16[128,4096]{1,0:T(8,128)(2,1)} %param.8) | copy-start | bytes 3145732
  11.6 92.7 %copy-start.10 = (f32[4096]{0:T(1024)S(1)}, f32[4096]{0:T(1024)}, u32[]{:S(2)}) copy-start(f32[4096]{0:T(1024)} %param.9) | copy-start | bytes 49156
  104.2 68.1 %copy-start.3 = (bf16[128,4096]{1,0:T(8,128)(2,1)S(1)}, bf16[128,4096]{1,0:T(8,128)(2,1)}, u32[]{:S(2)}) copy-start(bf16[128,4096]{1,0:T(8,128)(2,1)} %param.15) | copy-start | bytes 3145732
  109.4 65.4 %collective-permute-start = (bf16[2,3,256]{2,0,1:T(2,128)(2,1)S(1)}, bf16[2,3,256]{2,0,1:T(2,128)(2,1)S(1)}, u32[]{:S(2)}, u32[]{:S(2)}) collective-permute-start(bf16[2,3,256]{2,0,1:T(2,128)(2,1)S(1)} %bitcast.390), channel_id=1, source_target_pairs={{0,4},{4,8},{8,12},{12,16},{16,20},{20,24},{24,28},{28,32},{32,36}... | collective-permute-start | bytes 9224 | tf_op jit(solution)/shard_map/ppermute | solution.py:23
  174.4 1.0 copy-start.8
  174.4 1.0 copy-start.9
  176.4 23.9 %all-to-all-start = ((f32[3,256,128]{2,0,1:T(4,128)}), f32[3,256,128]{2,0,1:T(4,128)S(1)}, u32[]{:S(2)}, u32[]{:S(2)}) async-start(f32[3,256,128]{2,0,1:T(4,128)} %copy.176), calls=%async_computation | async-start | bytes 1048576 | tf_op jit(solution)/shard_map/all_to_all | solution.py:27
  183.0 113.3 %reduce-scatter.2.cloned.1.call-start = ((), (), s32[]{:S(2)}) async-start(), calls=%async_computation.5 | async-start | bytes 1310720 | tf_op jit(solution)/shard_map/reduce_scatter | solution.py:136
  217.0 53.8 %copy-start.12 = (f32[256]{0:T(256)S(1)}, f32[256]{0:T(256)}, u32[]{:S(2)}) copy-start(f32[256]{0:T(256)} %param.13) | copy-start | bytes 3076
  217.1 0.7 copy-start.7
  217.9 54.7 %copy-start.1 = (bf16[256,4096]{0,1:T(8,128)(2,1)S(1)}, bf16[256,4096]{0,1:T(8,128)(2,1)}, u32[]{:S(2)}) copy-start(bf16[256,4096]{0,1:T(8,128)(2,1)} %all-gather.5.cloned.1.call-done) | copy-start | bytes 6291460
  274.4 7.0 %copy-start.5 = (f32[128,1,256]{2,0,1:T(8,128)S(1)}, f32[128,1,256]{2,0,1:T(8,128)}, u32[]{:S(2)}) copy-start(f32[128,1,256]{2,0,1:T(8,128)} %get-tuple-element.5) | copy-start | bytes 393220
  274.4 7.0 %copy-start.6 = (f32[128,1,256]{2,0,1:T(8,128)S(1)}, f32[128,1,256]{2,0,1:T(8,128)}, u32[]{:S(2)}) copy-start(f32[128,1,256]{2,0,1:T(8,128)} %get-tuple-element.13) | copy-start | bytes 393220
  274.4 89.1 %all-reduce.2.cloned.1.call-start = ((), (), s32[]{:S(2)}) async-start(), calls=%async_computation.6 | async-start | bytes 4194304 | tf_op jit(solution)/shard_map/psum | solution.py:154
  276.5 4.9 %collective-permute-start.1 = (f32[2,3,256]{2,0,1:T(2,128)S(1)}, f32[2,3,256]{2,0,1:T(2,128)S(1)}, u32[]{:S(2)}, u32[]{:S(2)}) collective-permute-start(f32[2,3,256]{2,0,1:T(2,128)S(1)} %slice.110), channel_id=1, source_target_pairs={{4,0},{8,4},{12,8},{16,12},{20,16},{24,20},{28,24},{32,28},{36,32}... | collective-permute-start | bytes 18440 | tf_op jit(solution)/shard_map/ppermute | solution.py:23
  288.0 75.5 %copy-start.11 = (f32[4096]{0:T(1024)S(1)}, f32[4096]{0:T(1024)}, u32[]{:S(2)}) copy-start(f32[4096]{0:T(1024)} %param.9) | copy-start | bytes 49156
  291.1 74.5 %copy-start.4 = (bf16[128,4096]{1,0:T(8,128)(2,1)S(1)}, bf16[128,4096]{1,0:T(8,128)(2,1)}, u32[]{:S(2)}) copy-start(bf16[128,4096]{1,0:T(8,128)(2,1)} %param.15) | copy-start | bytes 3145732
  291.1 74.5 %copy-start.13 = (f32[128]{0:T(128)S(1)}, f32[128]{0:T(128)}, u32[]{:S(2)}) copy-start(f32[128]{0:T(128)} %get-tuple-element.18) | copy-start | bytes 1540
  291.1 74.5 %copy-start.15 = (f32[128]{0:T(128)S(1)}, f32[128]{0:T(128)}, u32[]{:S(2)}) copy-start(f32[128]{0:T(128)} %copy-done.14) | copy-start | bytes 1540
  363.5 2.2 copy-start.2
Sparse Core Ops, SparseCore 0:
  10.8 84.6 all-gather.2
  98.3 74.0 all-gather.4
  274.5 21.6 reduce-scatter.1
  298.5 64.9 all-reduce.1
